TPU v7x, 32 devices: a whole 2x2x4 slice. The times are simulated.
32 devices in a mesh: req: 8 (over y, x, core), tp: 4 (over z).
Axes of the slice: x: 2, y: 2, z: 4, core: 2. Of those that a mesh axis runs over, the one named last changes fastest.
Arguments:
- queries: bfloat16 [1536, 2560], P('req', 'tp'), may hold values from -5 to 5
- new_keys: bfloat16 [1536, 512], P('req', 'tp'), may hold values from -5 to 5
- new_values: bfloat16 [1536, 512], P('req', 'tp'), may hold values from -5 to 5
- key_pages: bfloat16 [512, 64, 512], P('req', None, 'tp'), may hold values from -5 to 5
- value_pages: bfloat16 [512, 64, 512], P('req', None, 'tp'), may hold values from -5 to 5
- page_table: int32 [32, 16], P('req'), may hold values from 0 to 511, as said below
- cache_lengths: int32 [32], P('req'), may hold values from 2 to 1024, as said below
- parents: int32 [32, 48], P('req'), may hold values from -1 to 46, as said below
- residual: bfloat16 [1536, 2560], P('req'), may hold values from -6 to 6
- out_weight: bfloat16 [2560, 2560], P('tp'), may hold values from -0.125 to 0.125
- norm_gain: float32 [2560], replicated, may hold values from 0.1 to 1.9
- router_weight: float32 [2560, 16], replicated, may hold values from -0.125 to 0.125
- routes: int32 [1536, 6], P('req'), may hold values from 0 to 15, all different within a row; in each aligned block of 192 rows (0 to 191, 192 to 383, ...) at most 91 rows name the same one
- expert_gate_up: bfloat16 [16, 2560, 2, 1536], P('req', None, None, 'tp'), may hold values from -0.125 to 0.125
- expert_down: bfloat16 [16, 1536, 2560], P('req', 'tp'), may hold values from -0.15625 to 0.15625
- shared_gate_up: bfloat16 [2560, 2, 1536], P(None, None, 'tp'), may hold values from -0.125 to 0.125
- shared_down: bfloat16 [1536, 2560], P('tp'), may hold values from -0.15625 to 0.15625
Outputs:
- layer_out: bfloat16 [1536, 2560], P('req', 'tp')
Inputs may be any that keep to these rules, and one draw needn't show every extreme that they name: `page_table`: the pages of the 4 requests of the d-th block of 4 rows are the d-th block of 64 pages of the pool, each named once. `cache_lengths`: some request holds 1024 positions. parents[r, 0] = -1, and 0 <= parents[r, i] < i for i >= 1. `routes`: A token's 6 experts differ. In each aligned block of 192 rows no expert is named by more than 91 rows, and in some block one expert is named by exactly 91.
All inputs are finite; a program needn't handle non-finite values.
Results may differ from a plain program's by a relative error of at most 0.02.
Values may be sent and summed in bfloat16 or wider, within the bound.
No kernel may reach another device: no remote copies, remote signals or barrier semaphores. Data moves between devices by JAX's collectives and lax.ppermute only.
A program may use at most 128 MiB of HBM per device.

v0:
```python
import math
import jax
import jax.numpy as jnp
from jax import lax
from jax.sharding import PartitionSpec as P

QH = 20
KVH = 4
HD = 128
EPSILON = 1e-06
NEGATIVE = -1e30


def rounded(values):
    return lax.optimization_barrier(values.astype(jnp.bfloat16)).astype(jnp.float32)


def ancestors(parents):
    tree_size = parents.shape[-1]
    position = jnp.arange(tree_size, dtype=jnp.int32)
    adjacency = (parents[..., :, None] == position[None, :]) | (
        position[:, None] == position[None, :]
    )
    closure = adjacency.astype(jnp.float32)
    for doubling in range(max(1, (tree_size - 1).bit_length())):
        closure = jnp.minimum(
            jnp.einsum("...ij,...jk->...ik", closure, closure, precision=lax.Precision.HIGHEST), 1.0
        )
    return closure > 0.5


def tree_attention(queries, cache_keys, cache_values, new_keys, new_values, lengths, allowed):
    scaling = 1.0 / math.sqrt(queries.shape[-1])
    cache_scores = (
        jnp.einsum("rtkgd,rckd->rkgtc", queries, cache_keys, preferred_element_type=jnp.float32)
        * scaling
    )
    tree_scores = (
        jnp.einsum("rtkgd,rskd->rkgts", queries, new_keys, preferred_element_type=jnp.float32)
        * scaling
    )
    live = jnp.arange(cache_keys.shape[1], dtype=jnp.int32)[None, :] < lengths[:, None]
    cache_scores = jnp.where(live[:, None, None, None, :], cache_scores, NEGATIVE)
    tree_scores = jnp.where(allowed[:, None, None, :, :], tree_scores, NEGATIVE)
    highest = jnp.maximum(jnp.max(cache_scores, axis=-1), jnp.max(tree_scores, axis=-1))[..., None]
    cache_exp = jnp.exp(cache_scores - highest)
    tree_exp = jnp.exp(tree_scores - highest)
    denominator = (jnp.sum(cache_exp, axis=-1) + jnp.sum(tree_exp, axis=-1))[..., None]
    cache_probs = (cache_exp / denominator).astype(jnp.bfloat16)
    tree_probs = (tree_exp / denominator).astype(jnp.bfloat16)
    mixed = jnp.einsum(
        "rkgtc,rckd->rtkgd", cache_probs, cache_values, preferred_element_type=jnp.float32
    )
    mixed = mixed + jnp.einsum(
        "rkgts,rskd->rtkgd", tree_probs, new_values, preferred_element_type=jnp.float32
    )
    return mixed.astype(jnp.bfloat16).reshape(queries.shape[0], queries.shape[1], -1)


def place_rows(routes, experts_local, groups, capacity):
    flat_expert = routes.reshape(-1)
    expert_ids = jnp.arange(experts_local * groups, dtype=jnp.int32)
    onehot = (flat_expert[:, None] == expert_ids[None, :]).astype(jnp.int32)
    earlier = jnp.cumsum(onehot, axis=0) - onehot
    rank = jnp.sum(earlier * onehot, axis=1)
    owner = flat_expert // experts_local
    local_expert = flat_expert % experts_local
    return (local_expert * groups + owner) * capacity + rank


def fill_outbox(row_values, slot_index, top_count, lead_shape):
    repeated = jnp.repeat(row_values, top_count, axis=0)
    outbox = jnp.zeros(
        (lead_shape[0] * lead_shape[1] * lead_shape[2], row_values.shape[1]), row_values.dtype
    )
    outbox = outbox.at[slot_index].set(repeated)
    return outbox.reshape(lead_shape + (row_values.shape[1],))


def shards(
    queries,
    new_keys,
    new_values,
    key_pages,
    value_pages,
    page_table,
    cache_lengths,
    parents,
    residual,
    out_weight,
    norm_gain,
    router_weight,
    routes,
    expert_gate_up,
    expert_down,
    shared_gate_up,
    shared_down,
):
    groups = lax.axis_size("req")
    tp_count = lax.axis_size("tp")
    requests = parents.shape[0]
    tree_size = parents.shape[1]
    row_count = requests * tree_size
    kv_local = new_keys.shape[1] // HD
    head_ratio = QH // KVH
    model_width = residual.shape[1]
    part_width = model_width // tp_count
    pages_dev = key_pages.shape[0]
    local_pages = page_table - lax.axis_index("req") * pages_dev
    cache_keys = key_pages[local_pages].reshape(requests, -1, kv_local, HD)
    cache_values = value_pages[local_pages].reshape(requests, -1, kv_local, HD)
    head_outputs = tree_attention(
        queries.reshape(requests, tree_size, kv_local, head_ratio, HD),
        cache_keys,
        cache_values,
        new_keys.reshape(requests, tree_size, kv_local, HD),
        new_values.reshape(requests, tree_size, kv_local, HD),
        cache_lengths,
        ancestors(parents),
    )
    attn_terms = jnp.dot(
        head_outputs.reshape(row_count, -1), out_weight, preferred_element_type=jnp.float32
    )
    column = lax.axis_index("tp") * part_width
    experts_local = expert_gate_up.shape[0]
    top_count = routes.shape[1]
    expert_count = experts_local * groups
    capacity = max(10 * requests, row_count * top_count * 5 // (4 * expert_count) + 1)
    slot_index = place_rows(routes, experts_local, groups, capacity)
    lead_shape = (experts_local, groups, capacity)
    attn_out = lax.psum(attn_terms.astype(jnp.bfloat16), "tp").astype(jnp.float32)
    hidden = rounded(residual.astype(jnp.float32) + attn_out)
    rstd = lax.rsqrt(jnp.mean(hidden * hidden, axis=1, keepdims=True) + EPSILON)
    normed = hidden * rstd * norm_gain
    logits = jnp.dot(normed, router_weight, precision=lax.Precision.HIGHEST)
    normed_bf = normed.astype(jnp.bfloat16)
    hidden_part = lax.dynamic_slice_in_dim(hidden, column, part_width, 1)
    outbox = fill_outbox(normed_bf, slot_index, top_count, lead_shape)
    arrived = lax.all_to_all(outbox, "req", split_axis=1, concat_axis=1, tiled=True)
    arrived = arrived.reshape(experts_local, groups * capacity, model_width)
    gate_up = jnp.einsum(
        "emd,edcf->emcf", arrived, expert_gate_up, preferred_element_type=jnp.float32
    )
    act = (jax.nn.silu(gate_up[:, :, 0]) * gate_up[:, :, 1]).astype(jnp.bfloat16)
    partial_value = rounded(
        jnp.einsum("emf,efd->emd", act, expert_down, preferred_element_type=jnp.float32)
    )
    summed = lax.psum_scatter(
        partial_value.astype(jnp.bfloat16), "tp", scatter_dimension=2, tiled=True
    )
    outputs = summed.reshape(experts_local, groups, capacity, part_width)
    returned = lax.all_to_all(outputs, "req", split_axis=1, concat_axis=1, tiled=True).reshape(
        -1, part_width
    )
    picked = returned[slot_index].astype(jnp.float32).reshape(row_count, top_count, part_width)
    expert_ids = jnp.arange(expert_count, dtype=jnp.int32)
    chosen = jnp.sum(
        jnp.where(routes[:, :, None] == expert_ids[None, None, :], logits[:, None, :], 0.0), axis=-1
    )
    gate_values = jax.nn.sigmoid(chosen)
    gate_values = gate_values / jnp.sum(gate_values, axis=1, keepdims=True)
    routed = jnp.sum(picked * gate_values[:, :, None], axis=1)
    shared_gu = jnp.einsum(
        "td,dcf->tcf", normed_bf, shared_gate_up, preferred_element_type=jnp.float32
    )
    shared_act = (jax.nn.silu(shared_gu[:, 0]) * shared_gu[:, 1]).astype(jnp.bfloat16)
    shared_terms = jnp.dot(shared_act, shared_down, preferred_element_type=jnp.float32)
    shared_out = lax.psum_scatter(
        shared_terms.astype(jnp.bfloat16), "tp", scatter_dimension=1, tiled=True
    ).astype(jnp.float32)
    return (hidden_part + shared_out + routed).astype(jnp.bfloat16)


def solution(mesh):
    in_specs = (
        P("req", "tp"),
        P("req", "tp"),
        P("req", "tp"),
        P("req", None, "tp"),
        P("req", None, "tp"),
        P("req", None),
        P("req"),
        P("req", None),
        P("req", None),
        P("tp", None),
        P(),
        P(),
        P("req", None),
        P("req", None, None, "tp"),
        P("req", "tp", None),
        P(None, None, "tp"),
        P("tp", None),
    )
    out_specs = P("req", "tp")
    return jax.shard_map(shards, mesh=mesh, in_specs=in_specs, out_specs=out_specs, check_vma=False)
```

profile of v0, /device:TPU:0, one launch (start us, length us, event | category | flops | bytes accessed | tf_op | source)
XLA Modules:
  0.0 486.2 jit_solution(5703992235077245131)
XLA Ops:
  6.6 0.8 compare_select_fusion.4
  7.5 0.8 iota_compare_fusion.5
  8.3 2.0 reshape.306
  10.2 1.0 convolution_minimum_fusion.5
  11.2 0.2 convolution_minimum_fusion.4
  11.5 0.2 convolution_minimum_fusion.3
  11.7 0.2 convolution_minimum_fusion.2
  11.9 0.2 convolution_minimum_fusion.1
  12.2 0.2 fusion.22
  12.4 0.1 copy.58
  12.5 2.9 gather_fusion.1
  15.4 2.1 bitcast_reduce_fusion
  17.6 0.4 fusion.55
  18.0 1.4 copy-done.2
  19.4 1.0 fusion.8
  20.4 0.1 fusion.28
  20.5 2.9 gather_fusion
  23.4 3.5 fusion.11
  26.9 0.3 fusion.21
  27.2 0.1 copy.61
  27.4 1.9 convolution_convert_fusion.2
  29.3 0.2 reduce-scatter.9.cloned.1.call-start
  29.6 0.1 copy.63
  29.7 0.1 eq.80
  29.8 0.1 eq.76
  30.0 0.1 reshape.311
  30.1 4.5 reduce-window.6
  34.7 0.4 slice_reduce_fusion
  35.1 0.2 reduce-window.9
  35.3 0.1 broadcast_add_fusion
  35.5 46.5 %all-reduce.2.cloned.1.call-done = bf16[192,2560]{1,0:T(8,128)(2,1)} async-done(((bf16[192,2560]{1,0:T(8,128)(2,1)}), bf16[192,2560]{1,0:T(8,128)(2,1)}) %all-reduce.2.cloned.1.call-update) | async-done | bytes 983056 | tf_op jit(solution)/shard_map/psum | solution.py:131
  82.0 1.7 add_convert_fusion
  83.7 0.3 multiply_reduce_fusion.1
  84.0 0.3 fusion.15
  84.3 4.0 broadcast_in_dim.72
  88.3 10.2 %reshape.347 = bf16[1152,2560]{1,0:T(8,128)(2,1)} reshape(bf16[192,6,2560]{2,1,0:T(8,128)(2,1)} %broadcast_in_dim.72) | data formatting | bytes 11796480 | tf_op jit(solution)/shard_map/reshape | solution.py:72
  98.5 17.2 %scatter_custom_fusion = bf16[1456,2560]{1,0:T(8,128)(2,1)} fusion(s32[1152]{0:T(1024)S(1)} %fusion.48, bf16[1152,2560]{1,0:T(8,128)(2,1)} %reshape.347, bf16[]{:T(256)} %constant.73.clone.1), kind=kCustom, calls=%fused_computation.18 | custom fusion | bytes 7455232 | tf_op jit(solution)/shard_map/scatter | solution.py:76
  115.7 6.3 %reshape.314 = bf16[2,8,91,2560]{3,2,1,0:T(8,128)(2,1)} reshape(bf16[1456,2560]{1,0:T(8,128)(2,1)} %scatter_custom_fusion) | data formatting | bytes 14909440 | tf_op jit(solution)/shard_map/reshape | solution.py:77
  121.9 27.5 %copy.66 = bf16[2,8,91,2560]{3,0,2,1:T(2,128)(2,1)S(1)} copy(bf16[2,8,91,2560]{3,2,1,0:T(8,128)(2,1)} %reshape.314) | data formatting | bytes 14909440 | tf_op jit(solution)/shard_map/reshape | solution.py:77
  149.4 87.5 %all_to_all.10 = bf16[2,8,91,2560]{3,0,2,1:T(2,128)(2,1)S(1)} all-to-all(bf16[2,8,91,2560]{3,0,2,1:T(2,128)(2,1)S(1)} %copy.66), channel_id=1, replica_groups=mesh['req'=8,'tp'=4] {'req'}, dimensions={1} | all-to-all | bytes 14909440 | tf_op jit(solution)/shard_map/all_to_all | solution.py:139
  236.9 9.0 %fusion = f32[2,728,2,384]{3,1,2,0:T(8,128)S(1)} fusion(bf16[2,2560,2,384]{3,2,1,0:T(2,128)(2,1)} %param.30, bf16[2,728,2560,1]{2,0,1,3:T(2,128)(2,1)S(1)} %bitcast.150), kind=kOutput, calls=%fused_computation.4 | convolution fusion | flops 5725224960 | bytes 19791872 | tf_op jit(solution)/shard_map/emd,edcf->emcf/dot_general | solution.py:141
  245.9 6.1 %convolution_convert_fusion = bf16[2,728,2560]{2,1,0:T(8,128)(2,1)} fusion(bf16[2,384,2560]{2,1,0:T(8,128)(2,1)S(1)} %copy-done.9, f32[2,728,2,384]{3,1,2,0:T(8,128)S(1)} %fusion), kind=kOutput, calls=%fused_computation.7 | convolution fusion | flops 2869694464 | bytes 15859712 | tf_op jit(solution)/shard_map/emf,efd->emd/dot_general | solution.py:146
  252.0 20.1 %copy.85 = bf16[2,728,2560]{1,0,2:T(2,128)(2,1)} copy(bf16[2,728,2560]{2,1,0:T(8,128)(2,1)} %convolution_convert_fusion) | data formatting | bytes 14909440
  272.1 18.3 %reshape.365 = bf16[2560,1456]{1,0:T(8,128)(2,1)} reshape(bf16[2560,2,728]{2,1,0:T(2,128)(2,1)} %bitcast.148) | data formatting | bytes 14909440
  290.5 0.3 reduce-scatter.7.cloned.1.call-start
  290.8 3.2 fusion.4
  294.0 0.7 convolution_convert_fusion.1
  294.7 1.4 copy.83
  296.1 128.2 %reduce-scatter.9.cloned.1.call-done = bf16[640,1456]{1,0:T(8,128)(2,1)} async-done(((bf16[2560,1456]{1,0:T(8,128)(2,1)}), bf16[640,1456]{1,0:T(8,128)(2,1)}) %reduce-scatter.9.cloned.1.call-update) | async-done | bytes 1863696
  424.4 5.2 %reshape.366 = bf16[640,2,728]{2,1,0:T(2,128)(2,1)S(1)} reshape(bf16[640,1456]{1,0:T(8,128)(2,1)} %reduce-scatter.9.cloned.1.call-done) | data formatting | bytes 3727360
  429.5 5.0 %copy.82 = bf16[2,728,640]{2,0,1:T(2,128)(2,1)} copy(bf16[2,728,640]{1,0,2:T(2,128)(2,1)S(1)} %bitcast.149) | data formatting | bytes 3727360 | tf_op jit(solution)/shard_map/reshape | solution.py:151
  434.5 3.8 all-to-all-start.1
  438.3 1.5 convert_element_type.77
  439.8 1.8 fusion.14
  441.7 0.8 copy.72
  442.4 16.1 %reduce-scatter.7.cloned.1.call-done = bf16[640,192]{1,0:T(8,128)(2,1)} async-done(((bf16[2560,192]{1,0:T(8,128)(2,1)}), bf16[640,192]{1,0:T(8,128)(2,1)}) %reduce-scatter.7.cloned.1.call-update) | async-done | bytes 245776
  458.5 1.1 copy.84
  459.7 2.7 all-to-all-done.1
  462.4 1.5 copy.71
  463.9 1.8 reshape.317
  465.8 4.8 gather_fusion.2
  470.6 4.0 reshape.318
  474.5 3.4 multiply_reduce_fusion
  477.9 1.8 add_convert_fusion.1
  (42 shorter events, 0.4 us)
Async XLA Ops:
  6.5 20.8 %copy-start = (bf16[640,2560]{1,0:T(8,128)(2,1)S(1)}, bf16[640,2560]{1,0:T(8,128)(2,1)}, u32[]{:S(2)}) copy-start(bf16[640,2560]{1,0:T(8,128)(2,1)} %param.26) | copy-start | bytes 9830404
  6.5 75.4 %all-reduce.2.cloned.1.call-start = ((), (), s32[]{:S(2)}) async-start(), calls=%async_computation.4 | async-start | bytes 1966080 | tf_op jit(solution)/shard_map/psum | solution.py:131
  11.9 5.6 %copy-start.6 = (bf16[192,128]{1,0:T(8,128)(2,1)S(1)}, bf16[192,128]{1,0:T(8,128)(2,1)}, u32[]{:S(2)}) copy-start(bf16[192,128]{1,0:T(8,128)(2,1)} %param.18) | copy-start | bytes 147460
  15.4 2.2 copy-start.3
  17.6 1.9 copy-start.2
  18.0 2.4 copy-start.4
  23.4 3.5 copy-start.5
  23.4 3.5 copy-start.12
  26.9 2.6 copy-start.7
  29.3 54.7 %copy-start.8 = (f32[2560]{0:T(1024)S(1)}, f32[2560]{0:T(1024)}, u32[]{:S(2)}) copy-start(f32[2560]{0:T(1024)} %param.27) | copy-start | bytes 30724
  29.3 395.0 %reduce-scatter.9.cloned.1.call-start = ((), (), s32[]{:S(2)}) async-start(), calls=%async_computation.6 | async-start | bytes 9830400
  236.9 9.0 %copy-start.9 = (bf16[2,384,2560]{2,1,0:T(8,128)(2,1)S(1)}, bf16[2,384,2560]{2,1,0:T(8,128)(2,1)}, u32[]{:S(2)}) copy-start(bf16[2,384,2560]{2,1,0:T(8,128)(2,1)} %param.31) | copy-start | bytes 11796484
  290.5 168.1 %reduce-scatter.7.cloned.1.call-start = ((), (), s32[]{:S(2)}) async-start(), calls=%async_computation.5 | async-start | bytes 1638400
  290.8 3.2 copy-start.10
  434.5 5.3 %copy-start.11 = (f32[2560,16]{0,1:T(8,128)S(1)}, f32[2560,16]{0,1:T(8,128)}, u32[]{:S(2)}) copy-start(f32[2560,16]{0,1:T(8,128)} %param.28) | copy-start | bytes 491524
  434.5 27.9 %all-to-all-start.1 = ((bf16[2,8,91,640]{3,0,2,1:T(2,128)(2,1)}), bf16[2,8,91,640]{3,0,2,1:T(2,128)(2,1)S(1)}, u32[]{:S(2)}, u32[]{:S(2)}) async-start(bf16[2,8,91,640]{3,0,2,1:T(2,128)(2,1)} %bitcast.151), calls=%async_computation.1 | async-start | bytes 3727360 | tf_op jit(solution)/shard_map/all_to_all | solution.py:152
  470.6 9.1 %copy-start.1 = (bf16[640,2560]{1,0:T(8,128)(2,1)S(1)}, bf16[640,2560]{1,0:T(8,128)(2,1)}, u32[]{:S(2)}) copy-start(bf16[640,2560]{1,0:T(8,128)(2,1)} %param.26) | copy-start | bytes 9830404
Sparse Core Ops, SparseCore 0:
  29.4 52.4 all-reduce.1
  290.6 133.7 reduce-scatter.8
  426.8 31.7 reduce-scatter.6
where the time goes:
time: 488 us; the launch traced here: 486 us
  waiting for transfers between devices  194 us (40%)
  local copies, waits for them, and re-layouts  140 us (29%)
  blocking collectives  87.5 us (18%)
  matrix products  31.1 us (6%)
  other arithmetic  16.7 us (3%)
  between operations  13.5 us (3%)
    unnamed x5, waiting for transfers between devices  144 us
    all_to_all x1, blocking collectives, shards(): lax.all_to_all(outbox, 'req', split_axis=1, concat_axis=1, tiled=True)  87.5 us
    unnamed x32, local copies, waits for them, and re-layouts  47.7 us
    psum x1, waiting for transfers between devices, shards(): lax.psum(attn_terms.astype(jnp.bfloat16), 'tp').astype(jnp.float32)  46.5 us
    reshape x2, local copies, waits for them, and re-layouts, fill_outbox(): return outbox.reshape(lead_shape + (row_values.shape[1],))  33.8 us
    scatter x1, local copies, waits for them, and re-layouts, fill_outbox(): outbox = outbox.at[slot_index].set(repeated)  17.2 us
    reshape x1, local copies, waits for them, and re-layouts, fill_outbox(): repeated = jnp.repeat(row_values, top_count, axis=0)  10.2 us
  transfers between devices with their start and end apart: 4, of which 4 were waited for; matrix products, arithmetic and copies ran while one was open for 5% of the time, Pallas kernels for 0%

commit v1 on v0

--- a/solution.py
+++ b/solution.py
@@ -136,7 +136,9 @@
     normed_bf = normed.astype(jnp.bfloat16)
     hidden_part = lax.dynamic_slice_in_dim(hidden, column, part_width, 1)
     outbox = fill_outbox(normed_bf, slot_index, top_count, lead_shape)
-    arrived = lax.all_to_all(outbox, "req", split_axis=1, concat_axis=1, tiled=True)
+    pieces = jnp.split(outbox, lax.axis_size("req"), axis=1)
+    received = lax.all_to_all(jnp.stack(pieces), "req", 0, 0)
+    arrived = jnp.concatenate(received, axis=1)
     arrived = arrived.reshape(experts_local, groups * capacity, model_width)
     gate_up = jnp.einsum(
         "emd,edcf->emcf", arrived, expert_gate_up, preferred_element_type=jnp.float32

time: 488 us -> 507 us (1.039)
  local copies, waits for them, and re-layouts: 140 us -> 155 us
    another operation x1 -> x3, local copies, waits for them, and re-layouts: 1.97 us -> 36.1 us  [the longest x2 34.2 us: shards(): received = lax.all_to_all(jnp.stack(pieces), 'req', 0, 0)]
    reshape x2 -> x1, local copies, waits for them, and re-layouts: 33.8 us -> 6.25 us  [fill_outbox(): return outbox.reshape(lead_shape + (row_values.shape[1],))]
    unnamed x32 -> x41, local copies, waits for them, and re-layouts: 47.7 us -> 56.7 us
where the time goes in v1:
time: 507 us; the launch traced here: 505 us
  waiting for transfers between devices  194 us (38%)
  local copies, waits for them, and re-layouts  155 us (31%)
  blocking collectives  87.5 us (17%)
  matrix products  34.4 us (7%)
  other arithmetic  16.7 us (3%)
  between operations  13.5 us (3%)
    unnamed x5, waiting for transfers between devices  144 us
    all_to_all x1, blocking collectives, shards(): received = lax.all_to_all(jnp.stack(pieces), 'req', 0, 0)  87.5 us
    unnamed x41, local copies, waits for them, and re-layouts  56.7 us
    psum x1, waiting for transfers between devices, shards(): lax.psum(attn_terms.astype(jnp.bfloat16), 'tp').astype(jnp.float32)  46.5 us
    another operation x2, local copies, waits for them, and re-layouts, shards(): received = lax.all_to_all(jnp.stack(pieces), 'req', 0, 0)  34.2 us
    scatter x1, local copies, waits for them, and re-layouts, fill_outbox(): outbox = outbox.at[slot_index].set(repeated)  17.2 us
    dot_general x1, matrix products, shards(): jnp.einsum('emf,efd->emd', act, expert_down, preferred_element_type=jnp.f...  10.5 us
    reshape x1, local copies, waits for them, and re-layouts, fill_outbox(): repeated = jnp.repeat(row_values, top_count, axis=0)  10.2 us
  transfers between devices with their start and end apart: 4, of which 4 were waited for; matrix products, arithmetic and copies ran while one was open for 5% of the time, Pallas kernels for 0%

profile of v1, /device:TPU:0, one launch (start us, length us, event | category | flops | bytes accessed | tf_op | source)
XLA Modules:
  0.0 505.1 jit_solution(12956136291536164954)
XLA Ops:
  6.6 0.8 compare_select_fusion.4
  7.5 0.8 iota_compare_fusion.5
  8.3 2.0 reshape.306
  10.2 1.0 convolution_minimum_fusion.5
  11.2 0.2 convolution_minimum_fusion.4
  11.5 0.2 convolution_minimum_fusion.3
  11.7 0.2 convolution_minimum_fusion.2
  11.9 0.2 convolution_minimum_fusion.1
  12.2 0.2 fusion.22
  12.5 2.9 gather_fusion.1
  15.4 2.1 bitcast_reduce_fusion
  17.6 0.4 fusion.63
  18.0 1.4 copy-done.2
  19.4 1.0 fusion.8
  20.5 2.9 gather_fusion
  23.4 3.5 fusion.11
  26.9 0.3 fusion.21
  27.4 1.9 convolution_convert_fusion.2
  29.3 0.2 reduce-scatter.9.cloned.1.call-start
  30.1 4.5 reduce-window.6
  34.7 0.4 slice_reduce_fusion
  35.1 0.2 reduce-window.9
  35.5 46.5 %all-reduce.2.cloned.1.call-done = bf16[192,2560]{1,0:T(8,128)(2,1)} async-done(((bf16[192,2560]{1,0:T(8,128)(2,1)}), bf16[192,2560]{1,0:T(8,128)(2,1)}) %all-reduce.2.cloned.1.call-update) | async-done | bytes 983056 | tf_op jit(solution)/shard_map/psum | solution.py:131
  82.0 1.7 add_convert_fusion
  83.7 0.3 multiply_reduce_fusion.1
  84.0 0.3 fusion.15
  84.3 4.0 broadcast_in_dim.72
  88.3 10.2 %reshape.347 = bf16[1152,2560]{1,0:T(8,128)(2,1)} reshape(bf16[192,6,2560]{2,1,0:T(8,128)(2,1)} %broadcast_in_dim.72) | data formatting | bytes 11796480 | tf_op jit(solution)/shard_map/reshape | solution.py:72
  98.5 17.2 %scatter_custom_fusion = bf16[1456,2560]{1,0:T(8,128)(2,1)} fusion(s32[1152]{0:T(1024)S(1)} %fusion.56, bf16[1152,2560]{1,0:T(8,128)(2,1)} %reshape.347, bf16[]{:T(256)} %constant.73.clone.1), kind=kCustom, calls=%fused_computation.18 | custom fusion | bytes 7455232 | tf_op jit(solution)/shard_map/scatter | solution.py:76
  115.7 6.3 %reshape.314 = bf16[2,8,91,2560]{3,2,1,0:T(8,128)(2,1)} reshape(bf16[1456,2560]{1,0:T(8,128)(2,1)} %scatter_custom_fusion) | data formatting | bytes 14909440 | tf_op jit(solution)/shard_map/reshape | solution.py:77
  121.9 1.3 fusion.32
  123.2 1.3 fusion.31
  124.4 1.3 fusion.30
  125.7 1.3 fusion.29
  127.0 1.3 fusion.28
  128.3 1.3 fusion.27
  129.5 1.3 fusion.26
  130.8 1.4 fusion.25
  132.3 32.7 %copy.95 = bf16[8,2,1,91,2560]{4,1,3,2,0:T(2,128)(2,1)S(1)} copy(bf16[8,2,1,91,2560]{4,3,1,2,0:T(8,128)(2,1)S(1)} %fusion.25) | data formatting | bytes 14909440 | tf_op jit(solution)/shard_map/stack | solution.py:140
  165.0 87.5 %all_to_all.10 = bf16[8,2,1,91,2560]{4,1,3,2,0:T(2,128)(2,1)S(1)} all-to-all(bf16[8,2,1,91,2560]{4,1,3,2,0:T(2,128)(2,1)S(1)} %copy.95), channel_id=1, replica_groups=mesh['req'=8,'tp'=4] {'req'}, dimensions={0} | all-to-all | bytes 14909440 | tf_op jit(solution)/shard_map/all_to_all | solution.py:140
  252.5 7.9 %fusion = f32[2,728,2,384]{3,1,2,0:T(8,128)} fusion(bf16[2,2560,2,384]{3,2,1,0:T(2,128)(2,1)S(1)} %bitcast.209, bf16[2,728,2560,1]{2,0,1,3:T(2,128)(2,1)S(1)} %bitcast.198), kind=kOutput, calls=%fused_computation.4 | convolution fusion | flops 5725224960 | bytes 19791872 | tf_op jit(solution)/shard_map/emd,edcf->emcf/dot_general | solution.py:143
  260.4 10.5 %convolution_convert_fusion = bf16[2,728,2560]{2,1,0:T(8,128)(2,1)} fusion(bf16[2,384,2560]{2,1,0:T(8,128)(2,1)} %param.31, f32[2,728,2,384]{3,1,2,0:T(8,128)} %fusion), kind=kOutput, calls=%fused_computation.7 | convolution fusion | flops 2869694464 | bytes 15859712 | tf_op jit(solution)/shard_map/emf,efd->emd/dot_general | solution.py:148
  270.9 20.1 %copy.114 = bf16[2,728,2560]{1,0,2:T(2,128)(2,1)} copy(bf16[2,728,2560]{2,1,0:T(8,128)(2,1)} %convolution_convert_fusion) | data formatting | bytes 14909440
  290.9 18.3 %reshape.365 = bf16[2560,1456]{1,0:T(8,128)(2,1)} reshape(bf16[2560,2,728]{2,1,0:T(2,128)(2,1)} %bitcast.196) | data formatting | bytes 14909440
  309.3 0.3 reduce-scatter.7.cloned.1.call-start
  309.6 3.2 fusion.4
  312.8 0.7 convolution_convert_fusion.1
  313.5 1.4 copy.112
  315.0 128.2 %reduce-scatter.9.cloned.1.call-done = bf16[640,1456]{1,0:T(8,128)(2,1)} async-done(((bf16[2560,1456]{1,0:T(8,128)(2,1)}), bf16[640,1456]{1,0:T(8,128)(2,1)}) %reduce-scatter.9.cloned.1.call-update) | async-done | bytes 1863696
  443.2 5.2 %reshape.366 = bf16[640,2,728]{2,1,0:T(2,128)(2,1)S(1)} reshape(bf16[640,1456]{1,0:T(8,128)(2,1)} %reduce-scatter.9.cloned.1.call-done) | data formatting | bytes 3727360
  448.4 5.0 copy.111
  453.3 3.8 all-to-all-start.1
  457.1 1.5 convert_element_type.77
  458.6 1.8 fusion.14
  460.5 0.8 copy.101
  461.3 16.1 %reduce-scatter.7.cloned.1.call-done = bf16[640,192]{1,0:T(8,128)(2,1)} async-done(((bf16[2560,192]{1,0:T(8,128)(2,1)}), bf16[640,192]{1,0:T(8,128)(2,1)}) %reduce-scatter.7.cloned.1.call-update) | async-done | bytes 245776
  477.4 1.1 copy.113
  478.5 2.7 all-to-all-done.1
  481.3 1.5 copy.100
  482.8 1.8 reshape.317
  484.6 4.8 gather_fusion.2
  489.4 4.0 reshape.318
  493.4 3.4 multiply_reduce_fusion
  496.7 1.8 add_convert_fusion.1
  (53 shorter events, 1.4 us)
Async XLA Ops:
  6.5 20.8 %copy-start = (bf16[640,2560]{1,0:T(8,128)(2,1)S(1)}, bf16[640,2560]{1,0:T(8,128)(2,1)}, u32[]{:S(2)}) copy-start(bf16[640,2560]{1,0:T(8,128)(2,1)} %param.26) | copy-start | bytes 9830404
  6.5 75.4 %all-reduce.2.cloned.1.call-start = ((), (), s32[]{:S(2)}) async-start(), calls=%async_computation.4 | async-start | bytes 1966080 | tf_op jit(solution)/shard_map/psum | solution.py:131
  11.9 5.6 %copy-start.6 = (bf16[192,128]{1,0:T(8,128)(2,1)S(1)}, bf16[192,128]{1,0:T(8,128)(2,1)}, u32[]{:S(2)}) copy-start(bf16[192,128]{1,0:T(8,128)(2,1)} %param.18) | copy-start | bytes 147460
  15.4 2.2 copy-start.3
  17.6 1.9 copy-start.2
  18.0 2.4 copy-start.4
  23.4 3.5 copy-start.5
  23.4 3.5 copy-start.11
  26.9 2.6 copy-start.7
  29.3 54.7 %copy-start.8 = (f32[2560]{0:T(1024)S(1)}, f32[2560]{0:T(1024)}, u32[]{:S(2)}) copy-start(f32[2560]{0:T(1024)} %param.27) | copy-start | bytes 30724
  29.3 413.9 %reduce-scatter.9.cloned.1.call-start = ((), (), s32[]{:S(2)}) async-start(), calls=%async_computation.6 | async-start | bytes 9830400
  130.8 121.7 %slice-start = ((s8[7864320]{0:T(1024)(128)(4,1)}), s8[4194304]{0:T(1024)(128)(4,1)S(1)}, s32[]{:S(2)}) async-start(s8[7864320]{0:T(1024)(128)(4,1)} %bitcast.208), calls=%async_computation.7 | async-start | bytes 8388608
  132.3 120.2 %slice-start.1 = ((s8[7864320]{0:T(1024)(128)(4,1)}), s8[3670016]{0:T(1024)(128)(4,1)S(1)}, s32[]{:S(2)}) async-start(s8[7864320]{0:T(1024)(128)(4,1)} %bitcast.208), calls=%async_computation.8 | async-start | bytes 7340032
  309.3 168.1 %reduce-scatter.7.cloned.1.call-start = ((), (), s32[]{:S(2)}) async-start(), calls=%async_computation.5 | async-start | bytes 1638400
  309.6 3.2 copy-start.9
  453.3 5.3 %copy-start.10 = (f32[2560,16]{0,1:T(8,128)S(1)}, f32[2560,16]{0,1:T(8,128)}, u32[]{:S(2)}) copy-start(f32[2560,16]{0,1:T(8,128)} %param.28) | copy-start | bytes 491524
  453.3 27.9 %all-to-all-start.1 = ((bf16[2,8,91,640]{3,0,2,1:T(2,128)(2,1)}), bf16[2,8,91,640]{3,0,2,1:T(2,128)(2,1)S(1)}, u32[]{:S(2)}, u32[]{:S(2)}) async-start(bf16[2,8,91,640]{3,0,2,1:T(2,128)(2,1)} %bitcast.199), calls=%async_computation.1 | async-start | bytes 3727360 | tf_op jit(solution)/shard_map/all_to_all | solution.py:154
  489.4 9.1 %copy-start.1 = (bf16[640,2560]{1,0:T(8,128)(2,1)S(1)}, bf16[640,2560]{1,0:T(8,128)(2,1)}, u32[]{:S(2)}) copy-start(bf16[640,2560]{1,0:T(8,128)(2,1)} %param.26) | copy-start | bytes 9830404
Sparse Core Ops, SparseCore 0:
  29.4 52.4 all-reduce.1
  309.4 133.7 reduce-scatter.8
  445.6 31.7 reduce-scatter.6
